TPU v7x, 256 devices: a whole 4x4x8 slice. The times are simulated.
256 devices in a mesh: gx: 32 (over y, z_hi, core), gz: 8 (over z_lo, x).
Axes of the slice: x: 4, y: 4, z: 8 (z_hi: 4, z_lo: 2; z = z_hi * 2 + z_lo), core: 2. Of those that a mesh axis runs over, the one named last changes fastest.
Arguments:
- scalars: float32 [2, 4096, 128, 256], P(None, 'gx', 'gz'), may hold values from -6 to 6
- diffusivity: float32 [4096, 128, 256], P('gx', 'gz'), may hold values from 0.01 to 0.1
- reaction_rate: float32 [4096, 128, 256], P('gx', 'gz'), may hold values from 0.05 to 1
- block_inverse: float32 [2, 32, 128, 128], P(None, 'gx'), may hold values from 0 to 1
- block_response: float32 [2, 32, 128], P(None, 'gx'), may hold values from 0 to 1, as said below
- mean_profile: float32 [2, 256], replicated, may hold values from -4 to 4
- recycle_gain: float32 [2, 256], replicated, may hold values from 0.5 to 1.5
- station_index: int32 [1], replicated, may hold values from 0 to 4095
- span_shift: int32 [1], replicated, may hold values from 0 to 127
Outputs:
- transported: float32 [2, 4096, 128, 256], P(None, 'gx', 'gz')
Inputs may be any that keep to these rules, and one draw needn't show every extreme that they name: `block_response`: every entry is positive.
All inputs are finite; a program needn't handle non-finite values.
Results may differ from a plain program's by a relative error of at most 0.0003.
Values sent between devices are 32-bit elements; how exact they have to be, the bound alone decides.
No kernel may reach another device: no remote copies, remote signals or barrier semaphores. Data moves between devices by JAX's collectives and lax.ppermute only.
A program may use at most 64 MiB of HBM per device.

v0:
```python
import jax
import jax.numpy as jnp
from jax import lax
from jax.sharding import PartitionSpec as P

reaction_yields = (-1.0, 1.0)


def from_root(x, axis, root):
    mine = lax.axis_index(axis) == root
    return lax.psum(jnp.where(mine, x, jnp.zeros_like(x)), axis)


def with_halo(x, sides, width, wrap):
    for axis, dim in sides:
        devices, length = (lax.axis_size(axis), x.shape[dim])
        up = [(i, (i + 1) % devices) for i in range(devices if wrap else devices - 1)]
        down = [(j, i) for i, j in up]
        last = lax.slice_in_dim(x, length - width, length, axis=dim)
        first = lax.slice_in_dim(x, 0, width, axis=dim)
        before = lax.ppermute(last, axis, up)
        after = lax.ppermute(first, axis, down)
        x = jnp.concatenate([before, x, after], axis=dim)
    return x


def prefix(part, axis, combine, identity):
    place = lax.axis_index(axis)
    gathered = jax.tree.map(lambda a: lax.all_gather(a, axis), part)
    state = jax.tree.map(lambda a, e: jnp.zeros_like(a) + jnp.asarray(e, a.dtype), part, identity)

    def one(hop, state):
        return combine(
            state, jax.tree.map(lambda a: lax.dynamic_index_in_dim(a, hop, 0, False), gathered)
        )

    return lax.fori_loop(0, place, one, state)


def fourth_order(padded, dimension, length):

    def shifted(offset):
        return lax.slice_in_dim(padded, offset, offset + length, axis=dimension)

    return (
        -shifted(0) + 16.0 * shifted(1) - 30.0 * shifted(2) + 16.0 * shifted(3) - shifted(4)
    ) / 12.0


def make_inflow(station_plane, mean_profile, recycle_gain, span_shift):
    span_mean = jnp.mean(station_plane, axis=1, keepdims=True)
    rolled = jnp.roll(station_plane, span_shift[0], axis=1)
    return mean_profile[:, None, :] + recycle_gain[:, None, :] * (rolled - span_mean)


def explicit_part(stream_padded, span_padded, center, diffusivity, reaction_rate):
    wall_padded = jnp.pad(center, ((0, 0), (0, 0), (0, 0), (2, 2)))
    laplacian = fourth_order(stream_padded, 1, center.shape[1])
    laplacian = laplacian + fourth_order(span_padded, 2, center.shape[2])
    laplacian = laplacian + fourth_order(wall_padded, 3, center.shape[3])
    reaction = reaction_rate * jax.nn.softplus(center[0]) * jax.nn.softplus(center[1])
    source = jnp.stack([reaction_yields[0] * reaction, reaction_yields[1] * reaction])
    return center + diffusivity[None] * laplacian + source


def on_device(
    scalars,
    diffusivity,
    reaction_rate,
    block_inverse,
    block_response,
    mean_profile,
    recycle_gain,
    station_index,
    span_shift,
):
    plane_count = scalars.shape[1]
    span_cells = scalars.shape[2]
    stream_devices = lax.axis_size("gx")
    stream_rank = lax.axis_index("gx")
    span_rank = lax.axis_index("gz")
    owner_row = station_index[0] // plane_count
    local_plane = station_index[0] - owner_row * plane_count
    own_slice = lax.dynamic_index_in_dim(scalars, local_plane, 1, keepdims=False)
    arrived = from_root(own_slice, "gx", owner_row)
    station_plane = lax.all_gather(arrived, "gz", axis=1, tiled=True)
    inflow_full = make_inflow(station_plane, mean_profile, recycle_gain, span_shift)
    inflow = lax.dynamic_slice_in_dim(inflow_full, span_rank * span_cells, span_cells, 1)
    stream_padded = with_halo(scalars, (("gx", 1),), 2, False)
    edge_shape = (scalars.shape[0], 2, scalars.shape[2], scalars.shape[3])
    inlet_planes = jnp.broadcast_to(inflow[:, None], edge_shape)
    outlet_planes = jnp.broadcast_to(scalars[:, -1:], edge_shape)
    head_planes = jnp.where(stream_rank == 0, inlet_planes, stream_padded[:, :2])
    tail_planes = jnp.where(stream_rank == stream_devices - 1, outlet_planes, stream_padded[:, -2:])
    window = jnp.concatenate([head_planes, stream_padded[:, 2:-2], tail_planes], axis=1)
    span_padded = with_halo(scalars, (("gz", 2),), 2, True)
    explicit = explicit_part(window, span_padded, scalars, diffusivity, reaction_rate)
    local_part = jnp.einsum(
        "sij,sjzy->sizy", block_inverse[:, 0], explicit, precision=lax.Precision.HIGHEST
    )
    response = block_response[:, 0]
    exit_plane = local_part[:, -1]
    exit_ratio = response[:, -1]

    def compose(earlier_part, later_part):
        return (
            earlier_part[0] * later_part[0],
            later_part[0][:, None, None] * earlier_part[1] + later_part[1],
        )

    identity = (jnp.ones_like(exit_ratio), jnp.zeros_like(exit_plane))
    through, upstream_sum = prefix((exit_ratio, exit_plane), "gx", compose, identity)
    incoming = through[:, None, None] * inflow + upstream_sum
    return local_part + response[:, :, None, None] * incoming[:, None]


def solution(mesh):
    return jax.shard_map(
        on_device,
        mesh=mesh,
        in_specs=(
            P(None, "gx", "gz", None),
            P("gx", "gz", None),
            P("gx", "gz", None),
            P(None, "gx", None, None),
            P(None, "gx", None),
            P(),
            P(),
            P(),
            P(),
        ),
        out_specs=P(None, "gx", "gz", None),
        check_vma=False,
    )
```

profile of v0, /device:TPU:217, one launch (start us, length us, event | category | flops | bytes accessed | tf_op | source)
XLA Modules:
  0.0 334.0 jit_solution(15417572126514026074)
XLA Ops:
  6.5 1.6 fusion.48
  8.1 1.3 collective-permute-start
  9.4 3.8 %collective-permute-start.1 = (f32[2,2,16,256]{3,2,1,0:T(8,128)}, f32[2,2,16,256]{3,2,1,0:T(8,128)}, u32[]{:S(2)}, u32[]{:S(2)}) collective-permute-start(f32[2,2,16,256]{3,2,1,0:T(8,128)} %get-tuple-element.62), channel_id=1, source_target_pairs={{8,0},{16,8},{24,16},{32,24},{40,32},{48,40},{56,48},{64,56},{72,6... | collective-permute-start | bytes 196616 | tf_op jit(solution)/shard_map/ppermute | solution.py:22
  13.3 3.6 %fusion.47 = (f32[2,128,2,256]{3,2,1,0:T(2,128)}, f32[2,128,2,256]{3,2,1,0:T(2,128)}) fusion(f32[2,128,16,256]{3,2,1,0:T(8,128)} %param.11), kind=kLoop, calls=%fused_computation.82 | loop fusion | bytes 2097152 | tf_op jit(solution)/shard_map/slice | solution.py:20
  16.9 2.9 collective-permute-start.3
  21.1 1.4 slice_bitcast_fusion
  22.5 0.9 slice_reduce_fusion
  24.2 1.3 dynamic-slice
  26.3 137.6 %all-reduce.2 = (f32[2,16,256]{2,1,0:T(8,128)S(1)}, f32[64]{0:T(128)S(1)}) all-reduce(f32[2,16,256]{2,1,0:T(8,128)S(1)} %fusion.44, f32[64]{0:T(128)S(1)} %dynamic-update-slice), channel_id=1, replica_groups=mesh['gx'=32,'gz'=8] {'gx'}, use_global_device_ids=true, to_apply=%region_0.1 | all-reduce | flops 8256 | bytes 66048 | tf_op jit(solution)/shard_map/psum | solution.py:11
  163.9 22.5 %all_gather.9 = f32[2,128,256]{2,1,0:T(8,128)S(1)} all-gather(f32[2,16,256]{2,1,0:T(8,128)S(1)} %get-tuple-element.53), channel_id=1, replica_groups=mesh['gx'=32,'gz'=8] {'gz'}, dimensions={1}, use_global_device_ids=true | all-gather | bytes 294912 | tf_op jit(solution)/shard_map/all_gather | solution.py:86
  186.5 6.7 %multiply_bitcast_fusion = (f32[1,128,16,256]{3,2,1,0:T(8,128)S(1)}, f32[128,16,256]{2,1,0:T(8,128)}) fusion(f32[2,128,16,256]{3,2,1,0:T(8,128)} %param.11, f32[128,16,256]{2,1,0:T(8,128)} %param.13), kind=kLoop, calls=%fused_computation.64 | loop fusion | flops 7864320 | bytes 10485760 | tf_op jit(solution)/shard_map/stack | solution.py:62
  193.1 1.6 broadcast_multiply_fusion
  195.4 4.7 %constant_dynamic-update-slice_fusion.1 = f32[2,128,18,256]{3,2,1,0:T(8,128)} fusion(f32[2,128,16,256]{3,2,1,0:T(8,128)} %param.11), kind=kLoop, calls=%fused_computation.78 | loop fusion | bytes 8388608
  200.0 0.9 broadcast_select_fusion.1
  201.7 1.1 constant_dynamic-update-slice_fusion
  202.7 25.1 %fusion.8 = f32[2,128,16,256]{3,2,1,0:T(8,128)S(1)} fusion(f32[2,128,16,256]{3,2,1,0:T(8,128)} %param.11, f32[2,2,16,256]{3,2,1,0:T(8,128)S(1)} %broadcast_select_fusion, f32[2,2,16,256]{3,2,1,0:T(8,128)S(1)} %broadcast_select_fusion.1, f32[2,128,2,256]{3,2,1,0:T(2,128)S(1)} %collective-permute-done.2, ...), kind=kLoop, calls=%fused_computation.22 | loop fusion | flops 35651584 | bytes 23724032 | tf_op jit(solution)/shard_map/add | solution.py:63
  227.8 6.3 %fusion.29 = f32[2,128,16,256]{3,1,2,0:T(8,128)S(1)} fusion(f32[2,128,16,256]{3,2,1,0:T(8,128)S(1)} %fusion.8, f32[2,1,128,128]{3,2,1,0:T(8,128)S(1)} %copy-done), kind=kOutput, calls=%fused_computation.49 | convolution fusion | flops 1610612736 | bytes 8519680 | tf_op jit(solution)/shard_map/sij,sjzy->sizy/dot_general | solution.py:98
  234.2 2.0 copy-done.1
  237.0 56.6 %all-gather.4.cloned.1.call-done = f32[64,1,16,256]{3,2,1,0:T(8,128)} async-done(((f32[2,1,16,256]{3,2,1,0:T(8,128)}), f32[64,1,16,256]{3,2,1,0:T(8,128)}) %all-gather.4.cloned.1.call-update) | async-done | bytes 1048592 | tf_op jit(solution)/shard_map/all_gather | solution.py:29
  293.6 26.3 %while.12 = (s32[]{:T(128)}, f32[2]{0:T(128)S(1)}, f32[2,16,256]{2,1,0:T(8,128)S(1)}, s32[]{:T(128)}, f32[32,2]{1,0:T(8,128)S(1)}, /*index=5*/f32[32,2,16,256]{3,2,1,0:T(8,128)}, s32[]{:T(128)}, s32[]{:T(128)}, s32[]{:T(128)}) while((s32[]{:T(128)}, f32[2]{0:T(128)S(1)}, f32[2,16,256]{2,1,0:T(8,128)S(1)}, s32[]{:T(128)}, ...), condition=%wide.region_3.4_spmd, body=%wide.region_2.3_spmd.sunk | while | flops 16391 | bytes 98479 | solution.py:37
  294.5 0.8 bitcast_add_fusion.2
  295.3 0.8 bitcast_add_fusion.2
  296.2 0.8 bitcast_add_fusion.2
  297.0 0.8 bitcast_add_fusion.2
  297.9 0.8 bitcast_add_fusion.2
  298.7 0.8 bitcast_add_fusion.2
  299.6 0.8 bitcast_add_fusion.2
  300.4 0.8 bitcast_add_fusion.2
  301.3 0.8 bitcast_add_fusion.2
  302.1 0.8 bitcast_add_fusion.2
  302.9 0.8 bitcast_add_fusion.2
  303.8 0.8 bitcast_add_fusion.2
  304.6 0.8 bitcast_add_fusion.2
  305.5 0.8 bitcast_add_fusion.2
  306.3 0.8 bitcast_add_fusion.2
  307.2 0.8 bitcast_add_fusion.2
  308.0 0.8 bitcast_add_fusion.2
  308.9 0.8 bitcast_add_fusion.2
  309.7 0.8 bitcast_add_fusion.2
  310.6 0.8 bitcast_add_fusion.2
  311.4 0.8 bitcast_add_fusion.2
  313.1 0.8 bitcast_add_fusion.2
  314.0 0.8 bitcast_add_fusion.2
  315.7 0.8 bitcast_add_fusion.2
  316.5 0.8 bitcast_add_fusion.2
  319.1 0.8 bitcast_add_fusion.2
  320.0 2.7 multiply_add_fusion
  322.7 4.4 %copy.19 = f32[2,128,16,256]{3,2,1,0:T(8,128)} copy(f32[2,128,16,256]{3,1,2,0:T(8,128)S(1)} %multiply_add_fusion) | data formatting | bytes 8388608 | tf_op jit(solution)/shard_map/add | solution.py:114
  (67 shorter events, 7.9 us)
Async XLA Ops:
  6.5 221.3 %copy-start = (f32[2,1,128,128]{3,2,1,0:T(8,128)S(1)}, f32[2,1,128,128]{3,2,1,0:T(8,128)}, u32[]{:S(2)}) copy-start(f32[2,1,128,128]{3,2,1,0:T(8,128)} %param.14) | copy-start | bytes 393220
  6.5 287.1 %all-gather.4.cloned.1.call-start = ((), (), s32[]{:S(2)}) async-start(), calls=%async_computation | async-start | bytes 1081344 | tf_op jit(solution)/shard_map/all_gather | solution.py:29
  8.1 191.9 %collective-permute-start = (f32[2,2,16,256]{3,2,1,0:T(8,128)}, f32[2,2,16,256]{3,2,1,0:T(8,128)}, u32[]{:S(2)}, u32[]{:S(2)}) collective-permute-start(f32[2,2,16,256]{3,2,1,0:T(8,128)} %get-tuple-element.61), channel_id=1, source_target_pairs={{0,8},{8,16},{16,24},{24,32},{32,40},{40,48},{48,56},{56,64},{64,7... | collective-permute-start | bytes 196616 | tf_op jit(solution)/shard_map/ppermute | solution.py:21
  9.4 191.5 %collective-permute-start.1 = (f32[2,2,16,256]{3,2,1,0:T(8,128)}, f32[2,2,16,256]{3,2,1,0:T(8,128)}, u32[]{:S(2)}, u32[]{:S(2)}) collective-permute-start(f32[2,2,16,256]{3,2,1,0:T(8,128)} %get-tuple-element.62), channel_id=1, source_target_pairs={{8,0},{16,8},{24,16},{32,24},{40,32},{48,40},{56,48},{64,56},{72,6... | collective-permute-start | bytes 196616 | tf_op jit(solution)/shard_map/ppermute | solution.py:22
  16.9 184.8 %collective-permute-start.3 = (f32[2,128,2,256]{3,2,1,0:T(2,128)}, f32[2,128,2,256]{3,2,1,0:T(2,128)S(1)}, u32[]{:S(2)}, u32[]{:S(2)}) collective-permute-start(f32[2,128,2,256]{3,2,1,0:T(2,128)} %get-tuple-element.59), channel_id=1, source_target_pairs={{1,0},{2,1},{3,2},{4,3},{5,4},{6,5},{7,6},{0,7},{9,8},{10,9},{11,1... | collective-permute-start | bytes 1572872 | tf_op jit(solution)/shard_map/ppermute | solution.py:22
  19.8 182.9 %collective-permute-start.2 = (f32[2,128,2,256]{3,2,1,0:T(2,128)}, f32[2,128,2,256]{3,2,1,0:T(2,128)S(1)}, u32[]{:S(2)}, u32[]{:S(2)}) collective-permute-start(f32[2,128,2,256]{3,2,1,0:T(2,128)} %get-tuple-element.60), channel_id=1, source_target_pairs={{0,1},{1,2},{2,3},{3,4},{4,5},{5,6},{6,7},{7,0},{8,9},{9,10},{10,1... | collective-permute-start | bytes 1572872 | tf_op jit(solution)/shard_map/ppermute | solution.py:21
  186.4 6.7 %copy-start.2 = (f32[128,16,256]{2,1,0:T(8,128)S(1)}, f32[128,16,256]{2,1,0:T(8,128)}, u32[]{:S(2)}) copy-start(f32[128,16,256]{2,1,0:T(8,128)} %param.12) | copy-start | bytes 6291460
  193.1 1.6 copy-start.3
  193.1 1.6 copy-start.4
  227.8 92.1 %copy-start.5 = (f32[2,1,128]{2,1,0:T(1,128)S(1)}, f32[2,1,128]{2,1,0:T(1,128)}, u32[]{:S(2)}) copy-start(f32[2,1,128]{2,1,0:T(1,128)} %param.15) | copy-start | bytes 3076
  234.2 2.0 copy-start.1
Sparse Core Ops, SparseCore 0:
  237.0 56.5 all-gather.3
where the time goes:
time: 337 us; the launch traced here: 334 us
  blocking collectives  160 us (47%)
  other arithmetic  65.5 us (19%)
  waiting for transfers between devices  56.6 us (17%)
  local copies, waits for them, and re-layouts  21.9 us (6%)
  between operations  15.5 us (5%)
  starting transfers between devices  8.06 us (2%)
  matrix products  6.35 us (2%)
    psum x1, blocking collectives, from_root(): return lax.psum(jnp.where(mine, x, jnp.zeros_like(x)), axis)  138 us
    all_gather x1, waiting for transfers between devices, prefix(): gathered = jax.tree.map(lambda a: lax.all_gather(a, axis), part)  56.6 us
    add x31, other arithmetic, compose(): later_part[0][:, None, None] * earlier_part[1] + later_part[1]  25.9 us
    add x1, other arithmetic, explicit_part(): return center + diffusivity[None] * laplacian + source  25.1 us
    all_gather x1, blocking collectives, on_device(): station_plane = lax.all_gather(arrived, 'gz', axis=1, tiled=True)  22.5 us
    unnamed x16, local copies, waits for them, and re-layouts  8.19 us
    ppermute x2, starting transfers between devices, with_halo(): after = lax.ppermute(first, axis, down)  6.77 us
  transfers between devices with their start and end apart: 5, of which 1 were waited for; matrix products, arithmetic and copies ran while one was open for 7% of the time, Pallas kernels for 0%

commit v1 on v0

--- a/solution.py
+++ b/solution.py
@@ -83,7 +83,10 @@
     local_plane = station_index[0] - owner_row * plane_count
     own_slice = lax.dynamic_index_in_dim(scalars, local_plane, 1, keepdims=False)
     arrived = from_root(own_slice, "gx", owner_row)
-    station_plane = lax.all_gather(arrived, "gz", axis=1, tiled=True)
+    count = lax.axis_size("gz")
+    blocks = jnp.stack([arrived for _ in range(count)])
+    blocks = lax.all_to_all(blocks, "gz", split_axis=0, concat_axis=0)
+    station_plane = jnp.concatenate(blocks, axis=1)
     inflow_full = make_inflow(station_plane, mean_profile, recycle_gain, span_shift)
     inflow = lax.dynamic_slice_in_dim(inflow_full, span_rank * span_cells, span_cells, 1)
     stream_padded = with_halo(scalars, (("gx", 1),), 2, False)

time: 337 us -> 309 us (0.917)
  blocking collectives: 160 us -> 138 us
  waiting for transfers between devices: 56.6 us -> 50.1 us
  starting transfers between devices: 8.06 us -> 12.4 us
    all_gather x1 -> x0, blocking collectives: 22.5 us -> none  [on_device(): station_plane = lax.all_gather(arrived, 'gz', axis=1, tiled=True)]
    all_gather x1, waiting for transfers between devices: 56.6 us -> 49.6 us  [prefix(): gathered = jax.tree.map(lambda a: lax.all_gather(a, axis), part)]
    all_to_all x0 -> x1, starting transfers between devices: none -> 4.48 us  [on_device(): blocks = lax.all_to_all(blocks, 'gz', split_axis=0, concat_axis=0)]
    unnamed x16 -> x18, local copies, waits for them, and re-layouts: 8.19 us -> 7.36 us
  transfers between devices with their start and end apart: 5 -> 6, of which waited for: 1 -> 2; matrix products, arithmetic and copies ran while one was open for 7% -> 6% of each run, Pallas kernels for 0% -> 0%
where the time goes in v1:
time: 309 us; the launch traced here: 306 us
  blocking collectives  138 us (45%)
  other arithmetic  63.2 us (20%)
  waiting for transfers between devices  50.1 us (16%)
  local copies, waits for them, and re-layouts  20.7 us (7%)
  between operations  15.6 us (5%)
  starting transfers between devices  12.4 us (4%)
  matrix products  6.35 us (2%)
    psum x1, blocking collectives, from_root(): return lax.psum(jnp.where(mine, x, jnp.zeros_like(x)), axis)  138 us
    all_gather x1, waiting for transfers between devices, prefix(): gathered = jax.tree.map(lambda a: lax.all_gather(a, axis), part)  49.6 us
    add x31, other arithmetic, compose(): later_part[0][:, None, None] * earlier_part[1] + later_part[1]  25.9 us
    add x1, other arithmetic, explicit_part(): return center + diffusivity[None] * laplacian + source  25 us
    unnamed x18, local copies, waits for them, and re-layouts  7.36 us
    another operation x1, other arithmetic, explicit_part(): jnp.stack([reaction_yields[0] * reaction, reaction_yields[1] * reaction])  6.69 us
    ppermute x2, starting transfers between devices, with_halo(): after = lax.ppermute(first, axis, down)  6.56 us
    dot_general x1, matrix products, on_device(): jnp.einsum('sij,sjzy->sizy', block_inverse[:, 0], explicit, precision=lax...  6.35 us
  transfers between devices with their start and end apart: 6, of which 2 were waited for; matrix products, arithmetic and copies ran while one was open for 6% of the time, Pallas kernels for 0%

profile of v1, /device:TPU:217, one launch (start us, length us, event | category | flops | bytes accessed | tf_op | source)
XLA Modules:
  0.0 306.2 jit_solution(1782909083492430511)
XLA Ops:
  7.3 0.9 slice_reduce_fusion
  8.1 1.3 dynamic-slice
  11.1 137.7 %all-reduce.2 = (f32[2,16,256]{2,1,0:T(8,128)S(1)}, f32[64]{0:T(128)S(1)}) all-reduce(f32[2,16,256]{2,1,0:T(8,128)S(1)} %get-tuple-element.61, f32[64]{0:T(128)S(1)} %dynamic-update-slice), channel_id=1, replica_groups=mesh['gx'=32,'gz'=8] {'gx'}, use_global_device_ids=true, to_apply=%region_0.1 | all-reduce | flops 8256 | bytes 66048 | tf_op jit(solution)/shard_map/psum | solution.py:11
  149.5 4.5 %all-to-all-start = ((f32[8,2,16,256]{3,2,1,0:T(8,128)}), f32[8,2,16,256]{3,2,1,0:T(8,128)S(1)}, u32[]{:S(2)}, u32[]{:S(2)}) async-start(f32[8,2,16,256]{3,2,1,0:T(8,128)} %stack.8), calls=%async_computation | async-start | bytes 524288 | tf_op jit(solution)/shard_map/all_to_all | solution.py:88
  154.0 0.9 fusion.47
  154.9 1.3 collective-permute-start
  156.2 3.0 collective-permute-start.1
  159.3 3.6 %fusion.46 = (f32[2,128,2,256]{3,2,1,0:T(2,128)}, f32[2,128,2,256]{3,2,1,0:T(2,128)}) fusion(f32[2,128,16,256]{3,2,1,0:T(8,128)} %param.11), kind=kLoop, calls=%fused_computation.82 | loop fusion | bytes 2097152 | tf_op jit(solution)/shard_map/slice | solution.py:20
  162.9 3.5 %collective-permute-start.3 = (f32[2,128,2,256]{3,2,1,0:T(2,128)}, f32[2,128,2,256]{3,2,1,0:T(2,128)}, u32[]{:S(2)}, u32[]{:S(2)}) collective-permute-start(f32[2,128,2,256]{3,2,1,0:T(2,128)} %get-tuple-element.59), channel_id=1, source_target_pairs={{1,0},{2,1},{3,2},{4,3},{5,4},{6,5},{7,6},{0,7},{9,8},{10,9},{11,1... | collective-permute-start | bytes 1572872 | tf_op jit(solution)/shard_map/ppermute | solution.py:22
  166.4 6.7 %multiply_bitcast_fusion = (f32[1,128,16,256]{3,2,1,0:T(8,128)S(1)}, f32[128,16,256]{2,1,0:T(8,128)}) fusion(f32[2,128,16,256]{3,2,1,0:T(8,128)} %param.11, f32[128,16,256]{2,1,0:T(8,128)} %param.13), kind=kLoop, calls=%fused_computation.64 | loop fusion | flops 7864320 | bytes 10485760 | tf_op jit(solution)/shard_map/stack | solution.py:62
  173.1 1.6 broadcast_multiply_fusion
  174.7 1.4 copy-done.1
  176.1 2.5 constant_dynamic-update-slice_fusion.1
  179.4 2.1 constant_dynamic-update-slice_fusion
  182.0 25.0 %fusion.8 = f32[2,128,16,256]{3,2,1,0:T(8,128)S(1)} fusion(f32[2,128,16,256]{3,2,1,0:T(8,128)} %param.11, f32[2,2,16,256]{3,2,1,0:T(8,128)S(1)} %broadcast_select_fusion, f32[2,2,16,256]{3,2,1,0:T(8,128)S(1)} %broadcast_select_fusion.1, f32[2,128,2,256]{3,2,1,0:T(2,128)S(1)} %collective-permute-done.2, ...), kind=kLoop, calls=%fused_computation.22 | loop fusion | flops 35651584 | bytes 23724032 | tf_op jit(solution)/shard_map/add | solution.py:63
  207.0 6.3 %fusion.29 = f32[2,128,16,256]{3,1,2,0:T(8,128)S(1)} fusion(f32[2,128,16,256]{3,2,1,0:T(8,128)S(1)} %fusion.8, f32[2,1,128,128]{3,2,1,0:T(8,128)S(1)} %copy-done), kind=kOutput, calls=%fused_computation.49 | convolution fusion | flops 1610612736 | bytes 8519680 | tf_op jit(solution)/shard_map/sij,sjzy->sizy/dot_general | solution.py:101
  213.4 2.0 copy-done.2
  216.1 49.6 %all-gather.4.cloned.1.call-done = f32[64,1,16,256]{3,2,1,0:T(8,128)} async-done(((f32[2,1,16,256]{3,2,1,0:T(8,128)}), f32[64,1,16,256]{3,2,1,0:T(8,128)}) %all-gather.4.cloned.1.call-update) | async-done | bytes 1048592 | tf_op jit(solution)/shard_map/all_gather | solution.py:29
  265.8 26.3 %while.12 = (s32[]{:T(128)}, f32[2]{0:T(128)S(1)}, f32[2,16,256]{2,1,0:T(8,128)S(1)}, s32[]{:T(128)}, f32[32,2]{1,0:T(8,128)S(1)}, /*index=5*/f32[32,2,16,256]{3,2,1,0:T(8,128)}, s32[]{:T(128)}, s32[]{:T(128)}, s32[]{:T(128)}) while((s32[]{:T(128)}, f32[2]{0:T(128)S(1)}, f32[2,16,256]{2,1,0:T(8,128)S(1)}, s32[]{:T(128)}, ...), condition=%wide.region_3.4_spmd, body=%wide.region_2.3_spmd.sunk | while | flops 16391 | bytes 98479 | solution.py:37
  266.6 0.8 bitcast_add_fusion.2
  267.5 0.8 bitcast_add_fusion.2
  268.3 0.8 bitcast_add_fusion.2
  269.2 0.8 bitcast_add_fusion.2
  270.0 0.8 bitcast_add_fusion.2
  270.9 0.8 bitcast_add_fusion.2
  271.7 0.8 bitcast_add_fusion.2
  272.6 0.8 bitcast_add_fusion.2
  273.4 0.8 bitcast_add_fusion.2
  274.3 0.8 bitcast_add_fusion.2
  275.1 0.8 bitcast_add_fusion.2
  276.0 0.8 bitcast_add_fusion.2
  276.8 0.8 bitcast_add_fusion.2
  277.7 0.8 bitcast_add_fusion.2
  278.5 0.8 bitcast_add_fusion.2
  279.4 0.8 bitcast_add_fusion.2
  280.2 0.8 bitcast_add_fusion.2
  281.0 0.8 bitcast_add_fusion.2
  281.9 0.8 bitcast_add_fusion.2
  282.7 0.8 bitcast_add_fusion.2
  283.6 0.8 bitcast_add_fusion.2
  284.4 0.8 bitcast_add_fusion.2
  285.3 0.8 bitcast_add_fusion.2
  286.1 0.8 bitcast_add_fusion.2
  287.8 0.8 bitcast_add_fusion.2
  288.7 0.8 bitcast_add_fusion.2
  291.2 0.8 bitcast_add_fusion.2
  292.1 2.7 multiply_add_fusion
  294.9 4.4 %copy.20 = f32[2,128,16,256]{3,2,1,0:T(8,128)} copy(f32[2,128,16,256]{3,1,2,0:T(8,128)S(1)} %multiply_add_fusion) | data formatting | bytes 8388608 | tf_op jit(solution)/shard_map/add | solution.py:117
  (71 shorter events, 7.0 us)
Async XLA Ops:
  6.5 200.4 %copy-start = (f32[2,1,128,128]{3,2,1,0:T(8,128)S(1)}, f32[2,1,128,128]{3,2,1,0:T(8,128)}, u32[]{:S(2)}) copy-start(f32[2,1,128,128]{3,2,1,0:T(8,128)} %param.14) | copy-start | bytes 393220
  149.5 29.7 %all-to-all-start = ((f32[8,2,16,256]{3,2,1,0:T(8,128)}), f32[8,2,16,256]{3,2,1,0:T(8,128)S(1)}, u32[]{:S(2)}, u32[]{:S(2)}) async-start(f32[8,2,16,256]{3,2,1,0:T(8,128)} %stack.8), calls=%async_computation | async-start | bytes 524288 | tf_op jit(solution)/shard_map/all_to_all | solution.py:88
  154.0 111.8 %all-gather.4.cloned.1.call-start = ((), (), s32[]{:S(2)}) async-start(), calls=%async_computation.1 | async-start | bytes 1081344 | tf_op jit(solution)/shard_map/all_gather | solution.py:29
  154.9 24.5 %collective-permute-start = (f32[2,2,16,256]{3,2,1,0:T(8,128)S(1)}, f32[2,2,16,256]{3,2,1,0:T(8,128)S(1)}, u32[]{:S(2)}, u32[]{:S(2)}) collective-permute-start(f32[2,2,16,256]{3,2,1,0:T(8,128)S(1)} %get-tuple-element.63), channel_id=1, source_target_pairs={{0,8},{8,16},{16,24},{24,32},{32,40},{40,48},{48,56},{56,64},{64,7... | collective-permute-start | bytes 196616 | tf_op jit(solution)/shard_map/ppermute | solution.py:21
  156.2 23.0 %collective-permute-start.1 = (f32[2,2,16,256]{3,2,1,0:T(8,128)S(1)}, f32[2,2,16,256]{3,2,1,0:T(8,128)S(1)}, u32[]{:S(2)}, u32[]{:S(2)}) collective-permute-start(f32[2,2,16,256]{3,2,1,0:T(8,128)S(1)} %get-tuple-element.64), channel_id=1, source_target_pairs={{8,0},{16,8},{24,16},{32,24},{40,32},{48,40},{56,48},{64,56},{72,6... | collective-permute-start | bytes 196616 | tf_op jit(solution)/shard_map/ppermute | solution.py:22
  162.9 16.5 %collective-permute-start.3 = (f32[2,128,2,256]{3,2,1,0:T(2,128)}, f32[2,128,2,256]{3,2,1,0:T(2,128)}, u32[]{:S(2)}, u32[]{:S(2)}) collective-permute-start(f32[2,128,2,256]{3,2,1,0:T(2,128)} %get-tuple-element.59), channel_id=1, source_target_pairs={{1,0},{2,1},{3,2},{4,3},{5,4},{6,5},{7,6},{0,7},{9,8},{10,9},{11,1... | collective-permute-start | bytes 1572872 | tf_op jit(solution)/shard_map/ppermute | solution.py:22
  166.4 6.7 %copy-start.3 = (f32[128,16,256]{2,1,0:T(8,128)S(1)}, f32[128,16,256]{2,1,0:T(8,128)}, u32[]{:S(2)}) copy-start(f32[128,16,256]{2,1,0:T(8,128)} %param.12) | copy-start | bytes 6291460
  166.4 15.5 %collective-permute-start.2 = (f32[2,128,2,256]{3,2,1,0:T(2,128)}, f32[2,128,2,256]{3,2,1,0:T(2,128)S(1)}, u32[]{:S(2)}, u32[]{:S(2)}) collective-permute-start(f32[2,128,2,256]{3,2,1,0:T(2,128)} %get-tuple-element.60), channel_id=1, source_target_pairs={{0,1},{1,2},{2,3},{3,4},{4,5},{5,6},{6,7},{7,0},{8,9},{9,10},{10,1... | collective-permute-start | bytes 1572872 | tf_op jit(solution)/shard_map/ppermute | solution.py:21
  173.1 2.9 copy-start.1
  176.1 3.3 %copy-start.4 = (f32[2,256]{1,0:T(2,128)S(1)}, f32[2,256]{1,0:T(2,128)}, u32[]{:S(2)}) copy-start(f32[2,256]{1,0:T(2,128)} %param.16) | copy-start | bytes 6148
  176.1 3.3 %copy-start.5 = (f32[2,256]{1,0:T(2,128)S(1)}, f32[2,256]{1,0:T(2,128)}, u32[]{:S(2)}) copy-start(f32[2,256]{1,0:T(2,128)} %param.17) | copy-start | bytes 6148
  207.0 85.1 %copy-start.6 = (f32[2,1,128]{2,1,0:T(1,128)S(1)}, f32[2,1,128]{2,1,0:T(1,128)}, u32[]{:S(2)}) copy-start(f32[2,1,128]{2,1,0:T(1,128)} %param.15) | copy-start | bytes 3076
  213.4 2.0 copy-start.2
Sparse Core Ops, SparseCore 0:
  216.2 49.5 all-gather.3
